TPU v7x, 128 devices: a whole 4x4x4 slice. The times are simulated.
128 devices in a mesh: req: 16 (over z, x), head: 8 (over y, core).
Axes of the slice: x: 4, y: 4, z: 4, core: 2. Of those that a mesh axis runs over, the one named last changes fastest.
Arguments:
- tokens: bfloat16 [256, 1280], P('req'), may hold values from -6 to 6
- w_qkv: bfloat16 [2, 3, 1280, 1280], P(None, None, 'head'), may hold values from -0.15625 to 0.15625
- w_out: bfloat16 [2, 1280, 1280], P(None, 'head'), may hold values from -0.15625 to 0.15625
- w_up: bfloat16 [2, 1280, 1280], P(None, 'head'), may hold values from -0.15625 to 0.15625
- w_down: bfloat16 [2, 1280, 1280], P(None, 'head'), may hold values from -0.15625 to 0.15625
- gain_attn: float32 [2, 1280], replicated, may hold values from 0.1 to 1.9
- gain_mlp: float32 [2, 1280], replicated, may hold values from 0.1 to 1.9
- suffix_cache: bfloat16 [2, 2, 512, 1280, 128], P(None, None, 'req', 'head'), may hold values from -110 to 110
- prompt_cache: bfloat16 [2, 2, 96, 1280, 128], P(None, None, 'req', 'head'), may hold values from -110 to 110
- suffix_table: int32 [16, 32], P('req'), may hold values from 0 to 31, each once within a row
- prompt_owner: int32 [96], replicated, may hold values from 0 to 95, each once
- suffix_len: int32 [256], P('req'), may hold values from 1 to 256, 32768 in all
- group_id: int32 [256], P('req'), may hold values from 0 to 23, never falling along the last dimension, each value on 1 to 16 neighbouring positions
Outputs:
- hidden: bfloat16 [256, 1280], P('req')
- new_cache: bfloat16 [2, 2, 256, 1280], P(None, None, 'req', 'head')
Inputs may be any that keep to these rules, and one draw needn't show every extreme that they name: `suffix_table`: each row holds every number once. `prompt_owner`: each number once. `group_id`: never falls from one request to the next; every group has 1 to 16 requests, one group exactly 16.
All inputs are finite; a program needn't handle non-finite values. No bound on the sum of `suffix_len` on one device may be relied on, other than what follows from the above.
Results may differ from a plain program's by a relative error of at most 0.019.
The roundings to bfloat16 on the way count: a program that leaves them out, or rounds other values in their place, can miss the bound.
Values may be sent and summed in bfloat16 or wider, within the bound.
No kernel may reach another device: no remote copies, remote signals or barrier semaphores. Data moves between devices by JAX's collectives and lax.ppermute only.
A program may use at most 128 MiB of HBM per device.

v0:
```python
import math
import jax
import jax.numpy as jnp
from jax import lax
from jax.sharding import PartitionSpec as P

HD = 80
PPAGES = 4
NEG_FLOOR = -1e30


def root_norm(values, gains):
    factor = lax.rsqrt(jnp.mean(values * values, axis=-1, keepdims=True) + 1e-06)
    return values * factor * gains


def page_groups(prompt_owner, count, page_len):
    owners = prompt_owner // PPAGES
    return jnp.repeat(owners, page_len, total_repeat_length=count * page_len)


def attend(
    query, key_new, val_new, layer_suffix, layer_prompt, pages, valid, group_id, prompt_owner
):
    row_count = query.shape[0]
    head_count = query.shape[1] // HD
    scale = 1.0 / math.sqrt(HD)
    page_len = layer_suffix.shape[3]
    own_pages = pages.shape[1]
    query_heads = query.reshape(row_count, head_count, HD)
    key_heads = key_new.reshape(row_count, head_count, HD)
    val_heads = val_new.reshape(row_count, head_count, HD)
    gathered_pages = layer_suffix[:, pages].reshape(
        2, row_count, own_pages, head_count, HD, page_len
    )
    scores = (
        jnp.einsum(
            "rhd,rphdt->rhpt", query_heads, gathered_pages[0], preferred_element_type=jnp.float32
        ).reshape(row_count, head_count, own_pages * page_len)
        * scale
    )
    own = (
        jnp.einsum("rhd,rhd->rh", query_heads, key_heads, preferred_element_type=jnp.float32)
        * scale
    )
    mask = valid[:, None, :]
    local_top = jnp.maximum(jnp.max(jnp.where(mask, scores, NEG_FLOOR), axis=-1), own)
    weights = jnp.exp(jnp.where(mask, scores - local_top[..., None], NEG_FLOOR))
    own_weight = jnp.exp(own - local_top)
    total = jnp.sum(weights, axis=-1) + own_weight
    weight_pages = weights.astype(jnp.bfloat16).reshape(row_count, head_count, own_pages, page_len)
    mixed = jnp.einsum(
        "rhpt,rphdt->rhd", weight_pages, gathered_pages[1], preferred_element_type=jnp.float32
    )
    mixed = mixed + jnp.einsum(
        "rh,rhd->rhd",
        own_weight.astype(jnp.bfloat16),
        val_heads,
        preferred_element_type=jnp.float32,
    )
    piece = lax.all_gather(layer_prompt, "req", axis=1, tiled=True)
    count = piece.shape[1]
    key_group = page_groups(prompt_owner, count, page_len)
    keys = piece[0].reshape(count, head_count, HD, page_len)
    vals = piece[1].reshape(count, head_count, HD, page_len)
    block = (
        jnp.einsum("rhd,phdt->rhpt", query_heads, keys, preferred_element_type=jnp.float32).reshape(
            row_count, head_count, count * page_len
        )
        * scale
    )
    match = (group_id[:, None] == key_group[None, :])[:, None, :]
    new_top = jnp.maximum(local_top, jnp.max(jnp.where(match, block, NEG_FLOOR), axis=-1))
    block_weights = jnp.exp(jnp.where(match, block - new_top[..., None], NEG_FLOOR))
    factor = jnp.exp(local_top - new_top)
    new_total = total * factor + jnp.sum(block_weights, axis=-1)
    block_rounded = block_weights.astype(jnp.bfloat16).reshape(
        row_count, head_count, count, page_len
    )
    new_mixed = mixed * factor[..., None] + jnp.einsum(
        "rhpt,phdt->rhd", block_rounded, vals, preferred_element_type=jnp.float32
    )
    return (new_mixed / new_total[..., None]).reshape(row_count, -1).astype(jnp.bfloat16)


def add_branch(residual, partial_value, gains, closing):
    residual = residual + lax.psum(partial_value, "head")
    if closing:
        normed = None
    else:
        normed = root_norm(residual, gains).astype(jnp.bfloat16)
    return (residual, normed)


def local(
    tokens,
    w_qkv,
    w_out,
    w_up,
    w_down,
    gain_attn,
    gain_mlp,
    suffix_cache,
    prompt_cache,
    suffix_table,
    prompt_owner,
    suffix_len,
    group_id,
):
    row_count = tokens.shape[0]
    layer_count = w_qkv.shape[0]
    width_here = w_qkv.shape[2]
    model_width = w_qkv.shape[3]
    pages = suffix_table[0].reshape(row_count, -1)
    span = pages.shape[1] * suffix_cache.shape[4]
    valid = jnp.arange(span, dtype=jnp.int32)[None, :] < suffix_len[:, None]
    whole = tokens.astype(jnp.float32)
    normed = root_norm(whole, gain_attn[0]).astype(jnp.bfloat16)
    residual = whole
    new_keys = []
    new_vals = []
    for layer in range(layer_count):
        projected = jnp.einsum(
            "rd,kd->rk",
            normed,
            w_qkv[layer].reshape(3 * width_here, model_width),
            preferred_element_type=jnp.float32,
        )
        projected = projected.reshape(row_count, 3, width_here).astype(jnp.bfloat16)
        query = projected[:, 0]
        key_new = projected[:, 1]
        val_new = projected[:, 2]
        new_keys.append(key_new)
        new_vals.append(val_new)
        attended = attend(
            query,
            key_new,
            val_new,
            suffix_cache[layer],
            prompt_cache[layer],
            pages,
            valid,
            group_id,
            prompt_owner,
        )
        partial_value = jnp.dot(attended, w_out[layer], preferred_element_type=jnp.float32)
        residual, normed = add_branch(residual, partial_value, gain_mlp[layer], False)
        hidden_units = jax.nn.silu(
            jnp.einsum("rd,fd->rf", normed, w_up[layer], preferred_element_type=jnp.float32)
        ).astype(jnp.bfloat16)
        partial_value = jnp.dot(hidden_units, w_down[layer], preferred_element_type=jnp.float32)
        closing = layer == layer_count - 1
        next_gains = gain_attn[layer] if closing else gain_attn[layer + 1]
        residual, normed = add_branch(residual, partial_value, next_gains, closing)
    hidden = residual.astype(jnp.bfloat16)
    new_cache = jnp.stack([jnp.stack(new_keys), jnp.stack(new_vals)], axis=1)
    return (hidden, new_cache)


def solution(mesh):
    placed = (
        P("req", None),
        P(None, None, "head", None),
        P(None, "head", None),
        P(None, "head", None),
        P(None, "head", None),
        P(),
        P(),
        P(None, None, "req", "head", None),
        P(None, None, "req", "head", None),
        P("req", None),
        P(),
        P("req"),
        P("req"),
    )
    return jax.shard_map(
        local,
        mesh=mesh,
        in_specs=placed,
        out_specs=(P("req", None), P(None, None, "req", "head")),
        check_vma=False,
    )
```

profile of v0, /device:TPU:1, one launch (start us, length us, event | category | flops | bytes accessed | tf_op | source)
XLA Modules:
  0.0 431.9 jit_solution(11187171101283764259)
XLA Ops:
  7.3 2.4 fusion.147
  11.4 0.7 reduce.26
  12.3 73.0 %gather_fusion.2 = s32[12288]{0:T(1024)S(1)} fusion(s32[96]{0:T(128)S(1)} %and_select_fusion, s32[12288]{0:T(1024)S(1)} %fusion.97), kind=kCustom, calls=%fused_computation.clone | custom fusion | bytes 147456 | tf_op jit(solution)/shard_map/jit(_take)/gather | solution.py:19
  85.4 4.6 %slice_bitcast_fusion = (bf16[2,32,160,128]{3,2,1,0:T(8,128)(2,1)S(1)}, bf16[2,32,160,128]{3,2,1,0:T(8,128)(2,1)}) fusion(bf16[2,2,32,160,128]{4,3,2,1,0:T(8,128)(2,1)} %param.26), kind=kLoop, calls=%fused_computation.11 | loop fusion | bytes 10485760 | tf_op jit(solution)/shard_map/squeeze | solution.py:139
  90.0 4.1 gather_fusion
  94.2 1.9 fusion.146
  97.3 3.6 fusion.144
  101.0 0.8 fusion.11
  102.3 1.2 fusion.62
  103.6 1.8 fusion.86
  105.5 0.7 all-gather.7.cloned.1.call-update
  106.3 2.4 gather_fusion.1
  108.8 3.0 fusion.145
  111.8 53.2 %all-reduce.5.cloned.1.call-done = f32[16,1280]{1,0:T(8,128)} async-done(((f32[16,1280]{1,0:T(8,128)}), f32[16,1280]{1,0:T(8,128)}) %all-reduce.5.cloned.1.call-update) | async-done | bytes 81936 | tf_op jit(solution)/shard_map/psum | solution.py:87
  165.0 1.0 multiply_reduce_fusion.2
  166.1 2.2 fusion.82
  168.3 67.2 %all-gather.7.cloned.1.call-done = bf16[1,2,96,160,128]{4,3,2,1,0:T(8,128)(2,1)} async-done(((bf16[1,2,6,160,128]{4,3,2,1,0:T(8,128)(2,1)}), bf16[1,2,96,160,128]{4,3,2,1,0:T(8,128)(2,1)}) %all-gather.7.cloned.1.call-update) | async-done | bytes 7864336 | tf_op jit(solution)/shard_map/all_gather | solution.py:61
  235.5 5.4 %fusion.143 = (bf16[1,1,96,160,128]{4,3,2,1,0:T(8,128)(2,1)}, bf16[1,1,96,160,128]{4,3,2,1,0:T(8,128)(2,1)}) fusion(bf16[1,2,96,160,128]{4,3,2,1,0:T(8,128)(2,1)} %all-gather.7.cloned.1.call-done), kind=kLoop, calls=%fused_computation.177 | loop fusion | bytes 15728640 | tf_op jit(solution)/shard_map/slice | solution.py:64
  241.0 52.7 %all-reduce.7.cloned.1.call-done = f32[16,1280]{1,0:T(8,128)} async-done(((f32[16,1280]{1,0:T(8,128)}), f32[16,1280]{1,0:T(8,128)}) %all-reduce.7.cloned.1.call-update) | async-done | bytes 81936 | tf_op jit(solution)/shard_map/psum | solution.py:87
  293.7 1.0 multiply_reduce_fusion.1
  294.7 1.7 fusion.41
  297.5 2.9 fusion.8
  300.4 1.7 fusion.20
  302.2 0.6 fusion.30
  302.7 3.3 fusion.65
  306.2 1.8 fusion.80
  308.1 56.1 %all-reduce.9.cloned.1.call-done = f32[16,1280]{1,0:T(8,128)} async-done(((f32[16,1280]{1,0:T(8,128)}), f32[16,1280]{1,0:T(8,128)}) %all-reduce.9.cloned.1.call-update) | async-done | bytes 81936 | tf_op jit(solution)/shard_map/psum | solution.py:87
  364.2 1.0 multiply_reduce_fusion
  365.2 2.2 fusion.76
  367.4 0.6 copy.45
  368.0 55.5 %all-reduce.11.cloned.1.call-done = f32[16,1280]{1,0:T(8,128)} async-done(((f32[16,1280]{1,0:T(8,128)}), f32[16,1280]{1,0:T(8,128)}) %all-reduce.11.cloned.1.call-update) | async-done | bytes 81936 | tf_op jit(solution)/shard_map/psum | solution.py:87
  423.5 1.5 add_convert_fusion
  (85 shorter events, 5.5 us)
Async XLA Ops:
  7.2 2.6 copy-start.4
  7.2 2.6 copy-start.2
  7.2 2.7 copy-start.3
  7.2 4.2 copy-start.8
  7.2 90.1 %all-gather.5.cloned.1.call-start = ((), (), s32[]{:S(2)}) async-start(), calls=%async_computation.4 | async-start | bytes 8355840 | tf_op jit(solution)/shard_map/all_gather | solution.py:61
  9.6 2.7 copy-start.9
  9.7 155.4 %all-reduce.5.cloned.1.call-start = ((), (), s32[]{:S(2)}) async-start(), calls=%async_computation | async-start | bytes 163840 | tf_op jit(solution)/shard_map/psum | solution.py:87
  90.0 4.2 copy-start.7
  94.2 2.5 copy-start.6
  105.5 130.1 %all-gather.7.cloned.1.call-start = ((), (), s32[]{:S(2)}) async-start(), calls=%async_computation.5 | async-start | bytes 8355840 | tf_op jit(solution)/shard_map/all_gather | solution.py:61
  106.2 187.5 %all-reduce.7.cloned.1.call-start = ((), (), s32[]{:S(2)}) async-start(), calls=%async_computation.1 | async-start | bytes 163840 | tf_op jit(solution)/shard_map/psum | solution.py:87
  106.2 2.5 copy-start.5
  108.7 57.3 %copy-start = (bf16[2,160,1280]{2,1,0:T(8,128)(2,1)S(1)}, bf16[2,160,1280]{2,1,0:T(8,128)(2,1)}, u32[]{:S(2)}) copy-start(bf16[2,160,1280]{2,1,0:T(8,128)(2,1)} %param.23) | copy-start | bytes 2457604
  168.3 125.4 %copy-start.1 = (f32[16,1280]{1,0:T(8,128)S(1)}, f32[16,1280]{1,0:T(8,128)}, u32[]{:S(2)}) copy-start(f32[16,1280]{1,0:T(8,128)} %all-reduce.5.cloned.1.call-done) | copy-start | bytes 245764
  168.3 195.9 %all-reduce.9.cloned.1.call-start = ((), (), s32[]{:S(2)}) async-start(), calls=%async_computation.2 | async-start | bytes 163840 | tf_op jit(solution)/shard_map/psum | solution.py:87
  308.0 115.5 %all-reduce.11.cloned.1.call-start = ((), (), s32[]{:S(2)}) async-start(), calls=%async_computation.3 | async-start | bytes 163840 | tf_op jit(solution)/shard_map/psum | solution.py:87
Sparse Core Ops, SparseCore 0:
  10.2 71.6 all-gather.4
  105.6 59.4 all-reduce.4
  167.2 68.3 all-gather.6
  237.7 55.9 all-reduce.6
  308.1 55.9 all-reduce.8
  367.5 55.9 all-reduce.10
where the time goes:
time: 433 us; the launch traced here: 432 us
  waiting for transfers between devices  286 us (66%)
  local copies, waits for them, and re-layouts  103 us (24%)
  matrix products  21.1 us (5%)
  between operations  14.4 us (3%)
  other arithmetic  7.59 us (2%)
    psum x4, waiting for transfers between devices, add_branch(): residual = residual + lax.psum(partial_value, 'head')  218 us
    gather x1, local copies, waits for them, and re-layouts, page_groups(): return jnp.repeat(owners, page_len, total_repeat_length=count * page_len)  73 us
    all_gather x2, waiting for transfers between devices, attend(): piece = lax.all_gather(layer_prompt, 'req', axis=1, tiled=True)  67.2 us
    slice x2, local copies, waits for them, and re-layouts, attend(): keys = piece[0].reshape(count, head_count, HD, page_len)  9.05 us
  transfers between devices with their start and end apart: 6, of which 5 were waited for; matrix products, arithmetic and copies ran while one was open for 24% of the time, Pallas kernels for 0%

commit v1 on v0

--- a/solution.py
+++ b/solution.py
@@ -84,7 +84,8 @@
 
 
 def add_branch(residual, partial_value, gains, closing):
-    residual = residual + lax.psum(partial_value, "head")
+    frames_order = lambda own_rows: lax.all_gather(own_rows, axis_name="head").sum(axis=0)
+    residual = residual + frames_order(partial_value)
     if closing:
         normed = None
     else:

time: 433 us -> 200 us (0.46)
  waiting for transfers between devices: 286 us -> 7.74 us
  blocking collectives: 0 us -> 56.1 us
  matrix products: 21.1 us -> 14 us
    psum x4 -> x0, waiting for transfers between devices: 218 us -> none  [add_branch(): residual = residual + lax.psum(partial_value, 'head')]
    all_gather x2, waiting for transfers between devices: 67.2 us -> 7.02 us  [attend(): piece = lax.all_gather(layer_prompt, 'req', axis=1, tiled=True)]
    all_gather x0 -> x4, blocking collectives: none -> 56.1 us  [add_branch(): lax.all_gather(own_rows, axis_name='head').sum(axis=0)]
    slice x2, local copies, waits for them, and re-layouts: 4.94 us -> 0.6 us  [attend(): gathered_pages[1]]
  transfers between devices with their start and end apart: 6 -> 2, of which waited for: 5 -> 1; matrix products, arithmetic and copies ran while one was open for 24% -> 53% of each run, Pallas kernels for 0% -> 0%
where the time goes in v1:
time: 200 us; the launch traced here: 199 us
  local copies, waits for them, and re-layouts  99.7 us (50%)
  blocking collectives  56.1 us (28%)
  between operations  14.4 us (7%)
  matrix products  14 us (7%)
  waiting for transfers between devices  7.74 us (4%)
  other arithmetic  7.09 us (4%)
    gather x1, local copies, waits for them, and re-layouts, page_groups(): return jnp.repeat(owners, page_len, total_repeat_length=count * page_len)  73 us
    all_gather x4, blocking collectives, add_branch(): lax.all_gather(own_rows, axis_name='head').sum(axis=0)  56.1 us
    slice x2, local copies, waits for them, and re-layouts, attend(): keys = piece[0].reshape(count, head_count, HD, page_len)  8.51 us
    all_gather x2, waiting for transfers between devices, attend(): piece = lax.all_gather(layer_prompt, 'req', axis=1, tiled=True)  7.02 us
    gather x2, local copies, waits for them, and re-layouts, attend(): layer_suffix[:, pages]  6.43 us
    dot_general x2, matrix products, attend(): jnp.einsum('rhpt,phdt->rhd', block_rounded, vals, preferred_element_type=...  4.6 us
    squeeze x1, local copies, waits for them, and re-layouts, local(): suffix_cache[layer]  4.48 us
  transfers between devices with their start and end apart: 2, of which 1 were waited for; matrix products, arithmetic and copies ran while one was open for 53% of the time, Pallas kernels for 0%

profile of v1, /device:TPU:1, one launch (start us, length us, event | category | flops | bytes accessed | tf_op | source)
XLA Modules:
  0.0 199.2 jit_solution(14645486540904505171)
XLA Ops:
  7.2 2.3 %fusion.147 = (bf16[1,2,6,160,128]{4,3,2,1,0:T(8,128)(2,1)}, bf16[1,2,6,160,128]{4,3,2,1,0:T(8,128)(2,1)}) fusion(bf16[2,2,6,160,128]{4,3,2,1,0:T(8,128)(2,1)} %param.27), kind=kLoop, calls=%fused_computation.181 | loop fusion | bytes 1966080 | tf_op jit(solution)/shard_map/slice | solution.py:141
  9.7 0.7 all-gather.11.cloned.1.call-update
  10.4 0.6 slice_reduce_fusion.1
  11.6 0.6 slice_bitcast_fusion.5
  13.2 0.7 reduce.26
  14.1 4.5 %slice_bitcast_fusion = (bf16[2,32,160,128]{3,2,1,0:T(8,128)(2,1)S(1)}, bf16[2,32,160,128]{3,2,1,0:T(8,128)(2,1)}) fusion(bf16[2,2,32,160,128]{4,3,2,1,0:T(8,128)(2,1)} %param.26), kind=kLoop, calls=%fused_computation.11 | loop fusion | bytes 10485760 | tf_op jit(solution)/shard_map/squeeze | solution.py:140
  18.6 4.1 %gather_fusion = bf16[32,2,160,128]{3,2,1,0:T(8,128)(2,1)} fusion(bf16[2,32,160,128]{3,2,1,0:T(8,128)(2,1)} %get-tuple-element.50, s32[1024]{0:T(1024)S(1)} %pad_clamp_fusion), kind=kCustom, calls=%fused_computation.1 | custom fusion | bytes 5243008 | tf_op jit(solution)/shard_map/gather | solution.py:33
  22.7 2.3 %gather_fusion.1 = bf16[32,2,160,128]{3,2,1,0:T(8,128)(2,1)} fusion(bf16[2,32,160,128]{3,2,1,0:T(8,128)(2,1)S(1)} %get-tuple-element.49, s32[1024]{0:T(1024)S(1)} %pad_clamp_fusion), kind=kCustom, calls=%fused_computation.2 | custom fusion | bytes 5243008 | tf_op jit(solution)/shard_map/gather | solution.py:33
  25.1 73.0 %gather_fusion.2 = s32[12288]{0:T(1024)S(1)} fusion(s32[96]{0:T(128)S(1)} %and_select_fusion, s32[12288]{0:T(1024)S(1)} %fusion.97), kind=kCustom, calls=%fused_computation.clone | custom fusion | bytes 147456 | tf_op jit(solution)/shard_map/jit(_take)/gather | solution.py:19
  98.2 0.6 slice_reduce_fusion
  100.4 0.6 copy-done
  101.3 3.7 %fusion.144 = (bf16[1,1,96,160,128]{4,3,2,1,0:T(8,128)(2,1)S(1)}, bf16[1,1,96,160,128]{4,3,2,1,0:T(8,128)(2,1)S(1)}) fusion(bf16[1,2,96,160,128]{4,3,2,1,0:T(8,128)(2,1)} %all-gather.9.cloned.1.call-done), kind=kLoop, calls=%fused_computation.178 | loop fusion | bytes 15728640 | tf_op jit(solution)/shard_map/slice | solution.py:64
  105.0 0.8 fusion.11
  105.8 0.5 fusion.28
  106.3 1.2 fusion.62
  107.7 1.2 fusion.86
  108.8 15.0 %all-gather.1 = f32[128,1280]{1,0:T(8,128)S(1)} all-gather(f32[16,1280]{1,0:T(8,128)S(1)} %fusion.86), channel_id=3, replica_groups=mesh['req'=16,'head'=8] {'head'}, dimensions={0}, use_global_device_ids=true | all-gather | bytes 737280 | tf_op jit(solution)/shard_map/all_gather | solution.py:87
  123.9 0.9 multiply_reduce_fusion.2
  124.8 2.3 %fusion.82 = f32[16,1280]{1,0:T(8,128)} fusion(bf16[2,160,1280]{2,1,0:T(8,128)(2,1)} %param.23, bf16[2,160,1280]{2,1,0:T(8,128)(2,1)} %param.22, f32[1280]{0:T(1024)} %get-tuple-element.30, f32[16]{0:T(128)S(1)} %add_rsqrt_fusion.2, f32[16,1280]{1,0:T(8,128)S(1)} %reduce_sum.111, bf16[16,1280]{1,0:T(8,128)(2,1)} %param.19), kind=kOutput, calls=%fused_computation.65 | convolution fusion | flops 13222400 | bytes 1032256 | tf_op jit(solution)/shard_map/dot_general | solution.py:152
  127.1 13.5 %all-gather.2 = f32[128,1280]{1,0:T(8,128)S(1)} all-gather(f32[16,1280]{1,0:T(8,128)} %fusion.82), channel_id=4, replica_groups=mesh['req'=16,'head'=8] {'head'}, dimensions={0}, use_global_device_ids=true | all-gather | bytes 737280 | tf_op jit(solution)/shard_map/all_gather | solution.py:87
  140.6 0.7 reduce_sum.113
  141.3 1.0 multiply_reduce_fusion.1
  142.3 1.8 fusion.41
  145.2 7.0 %all-gather.11.cloned.1.call-done = bf16[1,2,96,160,128]{4,3,2,1,0:T(8,128)(2,1)} async-done(((bf16[1,2,6,160,128]{4,3,2,1,0:T(8,128)(2,1)}), bf16[1,2,96,160,128]{4,3,2,1,0:T(8,128)(2,1)}) %all-gather.11.cloned.1.call-update) | async-done | bytes 7864336 | tf_op jit(solution)/shard_map/all_gather | solution.py:61
  152.2 4.8 %fusion.143 = (bf16[1,1,96,160,128]{4,3,2,1,0:T(8,128)(2,1)S(1)}, bf16[1,1,96,160,128]{4,3,2,1,0:T(8,128)(2,1)}) fusion(bf16[1,2,96,160,128]{4,3,2,1,0:T(8,128)(2,1)} %all-gather.11.cloned.1.call-done), kind=kLoop, calls=%fused_computation.177 | loop fusion | bytes 15728640 | tf_op jit(solution)/shard_map/slice | solution.py:64
  157.0 0.8 fusion.8
  158.3 0.6 fusion.30
  158.9 3.4 %fusion.65 = bf16[16,2,80]{2,0,1:T(8,128)(2,1)S(1)} fusion(bf16[96,2,80,128]{3,2,1,0:T(8,128)(2,1)} %bitcast.212, f32[2,16,96,128]{3,1,2,0:T(8,128)S(1)} %get-tuple-element.74, f32[16,2]{0,1:T(2,128)S(1)} %max.15, pred[16,96,128]{2,0,1:T(8,128)(4,1)S(1)} %broadcast_compare_fusion, f32[16,2,1,80,1]{3,2,4,1,0:T(1,128)S(1)} %fusion.20, ...), kind=kOutput, calls=%fused_computation.52 | convolution fusion | flops 64109568 | bytes 5727744 | tf_op jit(solution)/shard_map/rhpt,phdt->rhd/dot_general | solution.py:80
  162.6 14.4 %all-gather.4 = f32[128,1280]{1,0:T(8,128)S(1)} all-gather(f32[16,1280]{1,0:T(8,128)S(1)} %fusion.80), channel_id=6, replica_groups=mesh['req'=16,'head'=8] {'head'}, dimensions={0}, use_global_device_ids=true | all-gather | bytes 737280 | tf_op jit(solution)/shard_map/all_gather | solution.py:87
  177.7 13.2 %all-gather.5 = f32[128,1280]{1,0:T(8,128)S(1)} all-gather(f32[16,1280]{1,0:T(8,128)S(1)} %fusion.76), channel_id=7, replica_groups=mesh['req'=16,'head'=8] {'head'}, dimensions={0}, use_global_device_ids=true | all-gather | bytes 737280 | tf_op jit(solution)/shard_map/all_gather | solution.py:87
  191.0 0.6 add_convert_fusion
  191.7 0.6 copy.45
  (101 shorter events, 6.6 us)
Async XLA Ops:
  7.2 3.2 %copy-start.14 = (f32[2,1280]{1,0:T(2,128)S(1)}, f32[2,1280]{1,0:T(2,128)}, u32[]{:S(2)}) copy-start(f32[2,1280]{1,0:T(2,128)} %param.24) | copy-start | bytes 30724
  7.2 3.8 %copy-start.7 = (bf16[16,1280]{1,0:T(8,128)(2,1)S(1)}, bf16[16,1280]{1,0:T(8,128)(2,1)}, u32[]{:S(2)}) copy-start(bf16[16,1280]{1,0:T(8,128)(2,1)} %param.19) | copy-start | bytes 122884
  7.2 3.9 %copy-start.8 = (bf16[2,3,160,1280]{3,2,1,0:T(8,128)(2,1)S(1)}, bf16[2,3,160,1280]{3,2,1,0:T(8,128)(2,1)}, u32[]{:S(2)}) copy-start(bf16[2,3,160,1280]{3,2,1,0:T(8,128)(2,1)} %param.20) | copy-start | bytes 7372804
  7.2 94.1 %all-gather.9.cloned.1.call-start = ((), (), s32[]{:S(2)}) async-start(), calls=%async_computation | async-start | bytes 8355840 | tf_op jit(solution)/shard_map/all_gather | solution.py:61
  9.6 3.6 %copy-start.18 = (s32[1,32]{1,0:T(1,128)S(1)}, s32[1,32]{1,0:T(1,128)}, u32[]{:S(2)}) copy-start(s32[1,32]{1,0:T(1,128)} %param.28) | copy-start | bytes 388
  9.6 142.6 %all-gather.11.cloned.1.call-start = ((), (), s32[]{:S(2)}) async-start(), calls=%async_computation.1 | async-start | bytes 8355840 | tf_op jit(solution)/shard_map/all_gather | solution.py:61
  22.7 2.3 %copy-start.19 = (s32[96]{0:T(128)S(1)}, s32[96]{0:T(128)}, u32[]{:S(2)}) copy-start(s32[96]{0:T(128)} %param.29) | copy-start | bytes 1156
  25.1 73.1 %copy-start.15 = (f32[2,1280]{1,0:T(2,128)S(1)}, f32[2,1280]{1,0:T(2,128)}, u32[]{:S(2)}) copy-start(f32[2,1280]{1,0:T(2,128)} %param.25) | copy-start | bytes 30724
  25.1 73.7 %copy-start.17 = (s32[16]{0:T(128)S(1)}, s32[16]{0:T(128)}, u32[]{:S(2)}) copy-start(s32[16]{0:T(128)} %param.30) | copy-start | bytes 196
  25.1 73.8 %copy-start.1 = (bf16[32,2,160,128]{3,2,1,0:T(8,128)(2,1)S(1)}, bf16[32,2,160,128]{3,2,1,0:T(8,128)(2,1)}, u32[]{:S(2)}) copy-start(bf16[32,2,160,128]{3,2,1,0:T(8,128)(2,1)} %gather_fusion) | copy-start | bytes 7864324
  98.9 0.7 copy-start.9
  98.9 0.9 copy-start.16
  99.2 1.8 copy-start
  141.3 3.6 %copy-start.10 = (pred[16,2,128]{2,0,1:T(8,128)(4,1)S(1)}, pred[16,2,128]{2,0,1:T(8,128)(4,1)}, u32[]{:S(2)}) copy-start(pred[16,2,128]{2,0,1:T(8,128)(4,1)} %copy-done.9) | copy-start | bytes 12292
  142.3 14.7 %copy-start.5 = (f32[16,1280]{1,0:T(8,128)}, f32[16,1280]{1,0:T(8,128)S(1)}, u32[]{:S(2)}) copy-start(f32[16,1280]{1,0:T(8,128)S(1)} %get-tuple-element.40) | copy-start | bytes 245764
  158.9 3.5 %copy-start.4 = (bf16[2,160,1280]{2,1,0:T(8,128)(2,1)S(1)}, bf16[2,160,1280]{2,1,0:T(8,128)(2,1)}, u32[]{:S(2)}) copy-start(bf16[2,160,1280]{2,1,0:T(8,128)(2,1)} %param.21) | copy-start | bytes 2457604
  162.3 14.7 %copy-start.6 = (f32[16,1280]{1,0:T(8,128)S(1)}, f32[16,1280]{1,0:T(8,128)}, u32[]{:S(2)}) copy-start(f32[16,1280]{1,0:T(8,128)} %copy-done.5) | copy-start | bytes 245764
  162.3 14.9 %copy-start.2 = (bf16[2,160,1280]{2,1,0:T(8,128)(2,1)S(1)}, bf16[2,160,1280]{2,1,0:T(8,128)(2,1)}, u32[]{:S(2)}) copy-start(bf16[2,160,1280]{2,1,0:T(8,128)(2,1)} %param.23) | copy-start | bytes 2457604
  162.3 14.9 %copy-start.3 = (bf16[2,160,1280]{2,1,0:T(8,128)(2,1)S(1)}, bf16[2,160,1280]{2,1,0:T(8,128)(2,1)}, u32[]{:S(2)}) copy-start(bf16[2,160,1280]{2,1,0:T(8,128)(2,1)} %param.22) | copy-start | bytes 2457604
  162.3 14.9 %copy-start.11 = (f32[1280]{0:T(1024)S(1)}, f32[1280]{0:T(1024)}, u32[]{:S(2)}) copy-start(f32[1280]{0:T(1024)} %get-tuple-element.29) | copy-start | bytes 15364
  177.0 14.6 %copy-start.12 = (bf16[1,16,160]{2,1,0:T(8,128)(2,1)S(1)}, bf16[1,16,160]{2,1,0:T(8,128)(2,1)}, u32[]{:S(2)}) copy-start(bf16[1,16,160]{2,1,0:T(8,128)(2,1)} %get-tuple-element.61) | copy-start | bytes 15364
  177.1 14.6 %copy-start.13 = (bf16[1,16,160]{2,1,0:T(8,128)(2,1)S(1)}, bf16[1,16,160]{2,1,0:T(8,128)(2,1)}, u32[]{:S(2)}) copy-start(bf16[1,16,160]{2,1,0:T(8,128)(2,1)} %get-tuple-element.62) | copy-start | bytes 15364
Sparse Core Ops, SparseCore 0:
  10.1 71.6 all-gather.8
  84.0 68.1 all-gather.10
